TPU v7x, 32 devices: a whole 2x2x4 slice. The times are simulated.
32 devices in a mesh: fsdp: 8 (over y, x, core), dp: 4 (over z).
Axes of the slice: x: 2, y: 2, z: 4, core: 2. Of those that a mesh axis runs over, the one named last changes fastest.
Arguments:
- tokens: bfloat16 [131072, 1024], P(('fsdp', 'dp')), may hold values from -6 to 6
- cotangent: bfloat16 [131072, 1024], P(('fsdp', 'dp')), may hold values from -6 to 6
- lengths: int32 [256], P(('fsdp', 'dp')), may hold values from 8 to 2048, as said below
- selected: int32 [16384], P(('fsdp', 'dp')), may hold values from 0 to 4095, as said below
- attn_in: bfloat16 [1024, 3072], P('fsdp'), may hold values from -0.1875 to 0.1875
- attn_out: bfloat16 [1024, 1024], P('fsdp'), may hold values from -0.75 to 0.75
- mlp_in: bfloat16 [1024, 4096], P('fsdp'), may hold values from -0.1875 to 0.1875
- mlp_out: bfloat16 [4096, 1024], P('fsdp'), may hold values from -0.09375 to 0.09375
- norm_attn: bfloat16 [1024], P('fsdp'), may hold values from 0.5 to 1.5
- norm_mlp: bfloat16 [1024], P('fsdp'), may hold values from 0.5 to 1.5
- router: bfloat16 [1024], replicated, may hold values from -0.1875 to 0.1875
Outputs:
- output: bfloat16 [131072, 1024], P(('fsdp', 'dp'))
- grad_tokens: bfloat16 [131072, 1024], P(('fsdp', 'dp'))
- grad_attn_in: float32 [1024, 3072], P('fsdp')
- grad_attn_out: float32 [1024, 1024], P('fsdp')
- grad_mlp_in: float32 [1024, 4096], P('fsdp')
- grad_mlp_out: float32 [4096, 1024], P('fsdp')
- grad_norm_attn: float32 [1024], P('fsdp')
- grad_norm_mlp: float32 [1024], P('fsdp')
- grad_router: float32 [1024], replicated
Inputs may be any that keep to these rules, and one draw needn't show every extreme that they name: `lengths`: each aligned block of 8 entries (one device's sequences, in order) holds multiples of 8 that sum to 4096; exactly one of them equals 2048. `selected`: each aligned block of 512 entries lists distinct positions within its device's 4096 tokens in ascending order; a sequence of length L has exactly L / 8 of its positions listed.
All inputs are finite; a program needn't handle non-finite values.
Results may differ from a plain program's by a relative error of at most 0.014.
Values may be sent and summed in bfloat16 or wider, within the bound.
No kernel may reach another device: no remote copies, remote signals or barrier semaphores. Data moves between devices by JAX's collectives and lax.ppermute only.
A program may use at most 192 MiB of HBM per device.

v0:
```python
import numpy as np
import jax
import jax.numpy as jnp
from jax import lax
from jax.sharding import PartitionSpec as P

HEADS = 16
HEAD = 64
EPS = 1e-06
MASKED = -1e30


def rms_scale(values, gain_vec):
    return values * lax.rsqrt(jnp.mean(values * values, axis=-1, keepdims=True) + EPS) * gain_vec


def seq_mask(lengths, selected):
    seq_ends = jnp.cumsum(lengths)
    owner_seq = jnp.sum((selected[:, None] >= seq_ends[None, :]).astype(jnp.int32), axis=1)
    return (owner_seq[:, None] == owner_seq[None, :]) & (selected[None, :] <= selected[:, None])


def split_heads(matrix):
    return matrix.reshape(matrix.shape[0], HEADS, HEAD)


def masked_scores(query_heads, key_heads, allowed, score_scale):
    scores = (
        jnp.einsum("qhd,khd->hqk", query_heads, key_heads, preferred_element_type=jnp.float32)
        * score_scale
    )
    return jnp.where(allowed[None], scores, MASKED)


def plane_layout(mesh):
    devs = np.asarray(mesh.devices)
    if devs.ndim != 2 or devs.shape[0] != 8:
        return False
    try:
        for j in range(devs.shape[1]):
            for i in range(8):
                here = devs[i, j]
                mate = devs[i ^ 1, j]
                if (
                    tuple(mate.coords) != tuple(here.coords)
                    or mate.core_on_chip == here.core_on_chip
                ):
                    return False
                steps = []
                for bit in (2, 4):
                    other = devs[i ^ bit, j]
                    if other.core_on_chip != here.core_on_chip:
                        return False
                    diff = [abs(a - b) for a, b in zip(other.coords, here.coords)]
                    if sorted(diff) != [0] * (len(diff) - 1) + [1]:
                        return False
                    steps.append(diff.index(1))
                if steps[0] == steps[1]:
                    return False
    except AttributeError:
        return False
    return True


def swap_pairs(bit, size):
    return [(i, i ^ bit) for i in range(size)]


def plane_reduce(grad):
    rows, cols = grad.shape
    part = rows // 8
    half = part // 2
    me = lax.axis_index("fsdp")
    core = me % 2
    xi = me // 2 % 2
    yi = me // 4
    blocks = grad.reshape(4, 2, part, cols)
    keep = lax.dynamic_index_in_dim(blocks, core, axis=1, keepdims=False)
    send = lax.dynamic_index_in_dim(blocks, 1 - core, axis=1, keepdims=False)
    got = lax.ppermute(send.astype(jnp.bfloat16), "fsdp", swap_pairs(1, 8))
    chip = keep + got.astype(jnp.float32)

    def pick(y, x):
        return lax.dynamic_index_in_dim(chip, y * 2 + x, axis=0, keepdims=False)

    own = pick(yi, xi)
    to_x = pick(yi, 1 - xi)
    to_y = pick(1 - yi, xi)
    to_d = pick(1 - yi, 1 - xi)
    first_x = lax.ppermute(
        jnp.stack([to_x[:half], to_d[:half]]).astype(jnp.bfloat16), "fsdp", swap_pairs(2, 8)
    ).astype(jnp.float32)
    first_y = lax.ppermute(
        jnp.stack([to_y[half:], to_d[half:]]).astype(jnp.bfloat16), "fsdp", swap_pairs(4, 8)
    ).astype(jnp.float32)
    own_a = own[:half] + first_x[0]
    pass_a = to_y[:half] + first_x[1]
    own_b = own[half:] + first_y[0]
    pass_b = to_x[half:] + first_y[1]
    second_y = lax.ppermute(pass_a.astype(jnp.bfloat16), "fsdp", swap_pairs(4, 8)).astype(
        jnp.float32
    )
    second_x = lax.ppermute(pass_b.astype(jnp.bfloat16), "fsdp", swap_pairs(2, 8)).astype(
        jnp.float32
    )
    shard = jnp.concatenate([own_a + second_y, own_b + second_x], axis=0)
    return lax.psum(shard.astype(jnp.bfloat16), "dp").astype(jnp.float32)


def plain_reduce(grad):
    shard = lax.psum_scatter(grad.astype(jnp.bfloat16), "fsdp", scatter_dimension=0, tiled=True)
    return lax.psum(shard, "dp").astype(jnp.float32)


def make_per_device(reduce_grad):

    def per_device(
        tokens,
        cotangent,
        lengths,
        selected,
        attn_in,
        attn_out,
        mlp_in,
        mlp_out,
        norm_attn,
        norm_mlp,
        router,
    ):
        model_width = tokens.shape[1]
        row_count = selected.shape[0]
        score_scale = HEAD ** (-0.5)
        w_qkv, gain_attn = (
            lax.all_gather(attn_in, "fsdp", axis=0, tiled=True),
            lax.all_gather(norm_attn, "fsdp", axis=0, tiled=True),
        )
        w_out = lax.all_gather(attn_out, "fsdp", axis=0, tiled=True)
        w_in, gain_mlp = (
            lax.all_gather(mlp_in, "fsdp", axis=0, tiled=True),
            lax.all_gather(norm_mlp, "fsdp", axis=0, tiled=True),
        )
        w_down = lax.all_gather(mlp_out, "fsdp", axis=0, tiled=True)
        gain_one = gain_attn.astype(jnp.float32)
        gain_two = gain_mlp.astype(jnp.float32)
        positions = lax.broadcasted_iota(jnp.int32, (row_count, tokens.shape[0]), 1)
        select = (selected[:, None] == positions).astype(jnp.bfloat16)
        routed = jnp.dot(select, tokens, preferred_element_type=jnp.float32)
        routed_low = routed.astype(jnp.bfloat16)
        router_rate = jnp.dot(routed_low, router, preferred_element_type=jnp.float32)
        allowed = seq_mask(lengths, selected)
        normed_float, norm_pull = jax.vjp(rms_scale, routed, gain_one)
        normed = normed_float.astype(jnp.bfloat16)
        qkv = jnp.dot(normed, w_qkv, preferred_element_type=jnp.float32).astype(jnp.bfloat16)
        query_heads = split_heads(qkv[:, :model_width])
        key_heads = split_heads(qkv[:, model_width : 2 * model_width])
        value_heads = split_heads(qkv[:, 2 * model_width :])
        scores = masked_scores(query_heads, key_heads, allowed, score_scale)
        highest = jnp.max(scores, axis=-1, keepdims=True)
        exponent = jnp.exp(scores - highest)
        row_total = jnp.sum(exponent, axis=-1, keepdims=True)
        probabilities = (exponent / row_total).astype(jnp.bfloat16)
        log_total = highest + jnp.log(row_total)
        attn_mix = jnp.einsum(
            "hqk,khd->qhd", probabilities, value_heads, preferred_element_type=jnp.float32
        )
        attn_mix = attn_mix.reshape(row_count, model_width).astype(jnp.bfloat16)
        attended = jnp.dot(attn_mix, w_out, preferred_element_type=jnp.float32)
        middle = routed + attended
        normed_two_float, middle_pull = jax.vjp(rms_scale, middle, gain_two)
        normed_two = normed_two_float.astype(jnp.bfloat16)
        pre_gelu = jnp.dot(normed_two, w_in, preferred_element_type=jnp.float32)
        active_float, gelu_pull = jax.vjp(jax.nn.gelu, pre_gelu)
        active = active_float.astype(jnp.bfloat16)
        expanded = jnp.dot(active, w_down, preferred_element_type=jnp.float32)
        update = attended + expanded
        branch = (router_rate[:, None] * update).astype(jnp.bfloat16)
        output = (
            tokens.astype(jnp.float32)
            + jnp.einsum("kt,kd->td", select, branch, preferred_element_type=jnp.float32)
        ).astype(jnp.bfloat16)
        cot_rows = jnp.dot(select, cotangent, preferred_element_type=jnp.float32)
        grad_rate = jnp.sum(cot_rows * update, axis=-1)
        grad_update = cot_rows * router_rate[:, None]
        grad_expanded = grad_update.astype(jnp.bfloat16)
        grad_down = jnp.einsum(
            "kf,kd->fd", active, grad_expanded, preferred_element_type=jnp.float32
        )
        shard_down = reduce_grad(grad_down)
        grad_active = jnp.einsum(
            "kd,fd->kf", grad_expanded, w_down, preferred_element_type=jnp.float32
        )
        (grad_inner_float,) = gelu_pull(grad_active)
        grad_inner = grad_inner_float.astype(jnp.bfloat16)
        grad_up = jnp.einsum(
            "kd,kf->df", normed_two, grad_inner, preferred_element_type=jnp.float32
        )
        shard_up = reduce_grad(grad_up)
        grad_normed_two = jnp.einsum(
            "kf,df->kd", grad_inner, w_in, preferred_element_type=jnp.float32
        )
        grad_middle, grad_gain_two = middle_pull(grad_normed_two)
        grad_attended = (grad_update + grad_middle).astype(jnp.bfloat16)
        grad_proj = jnp.einsum(
            "ka,kd->ad", attn_mix, grad_attended, preferred_element_type=jnp.float32
        )
        shard_proj = reduce_grad(grad_proj)
        grad_mix = jnp.einsum(
            "kd,ad->ka", grad_attended, w_out, preferred_element_type=jnp.float32
        ).astype(jnp.bfloat16)
        grad_mix_heads = split_heads(grad_mix)
        scores_again = masked_scores(query_heads, key_heads, allowed, score_scale)
        prob_float = jnp.where(allowed[None], jnp.exp(scores_again - log_total), 0.0)
        grad_probs = jnp.einsum(
            "qhd,khd->hqk", grad_mix_heads, value_heads, preferred_element_type=jnp.float32
        )
        row_delta = jnp.sum(prob_float * grad_probs, axis=-1, keepdims=True)
        grad_scores = (prob_float * (grad_probs - row_delta)).astype(jnp.bfloat16)
        prob_low = prob_float.astype(jnp.bfloat16)
        grad_query = (
            jnp.einsum("hqk,khd->qhd", grad_scores, key_heads, preferred_element_type=jnp.float32)
            * score_scale
        )
        grad_key = (
            jnp.einsum("hqk,qhd->khd", grad_scores, query_heads, preferred_element_type=jnp.float32)
            * score_scale
        )
        grad_value = jnp.einsum(
            "hqk,qhd->khd", prob_low, grad_mix_heads, preferred_element_type=jnp.float32
        )
        grad_qkv = jnp.concatenate(
            [
                grad_query.reshape(row_count, model_width),
                grad_key.reshape(row_count, model_width),
                grad_value.reshape(row_count, model_width),
            ],
            axis=1,
        ).astype(jnp.bfloat16)
        grad_proj_in = jnp.einsum("kd,ke->de", normed, grad_qkv, preferred_element_type=jnp.float32)
        shard_qkv = reduce_grad(grad_proj_in)
        grad_normed = jnp.einsum("ke,de->kd", grad_qkv, w_qkv, preferred_element_type=jnp.float32)
        grad_routed_norm, grad_gain_one = norm_pull(grad_normed)
        grad_routed = (
            grad_routed_norm + grad_middle + grad_rate[:, None] * router.astype(jnp.float32)
        ).astype(jnp.bfloat16)
        grad_tokens = (
            cotangent.astype(jnp.float32)
            + jnp.einsum("kt,kd->td", select, grad_routed, preferred_element_type=jnp.float32)
        ).astype(jnp.bfloat16)
        router_local = jnp.dot(grad_rate, routed, precision=lax.Precision.HIGHEST)
        small = lax.psum(
            jnp.concatenate([grad_gain_one, grad_gain_two, router_local]), ("fsdp", "dp")
        )
        gain_part = grad_gain_one.shape[0] // lax.axis_size("fsdp")
        me = lax.axis_index("fsdp")
        shard_gain_one = lax.dynamic_slice_in_dim(small, me * gain_part, gain_part)
        shard_gain_two = lax.dynamic_slice_in_dim(
            small, grad_gain_one.shape[0] + me * gain_part, gain_part
        )
        grad_router = small[2 * grad_gain_one.shape[0] :]
        return (
            output,
            grad_tokens,
            shard_qkv,
            shard_proj,
            shard_up,
            shard_down,
            shard_gain_one,
            shard_gain_two,
            grad_router,
        )

    return per_device


def solution(mesh):
    placed = (
        P(("fsdp", "dp"), None),
        P(("fsdp", "dp"), None),
        P(("fsdp", "dp")),
        P(("fsdp", "dp")),
        P("fsdp", None),
        P("fsdp", None),
        P("fsdp", None),
        P("fsdp", None),
        P("fsdp"),
        P("fsdp"),
        P(),
    )
    reduce_grad = plane_reduce if plane_layout(mesh) else plain_reduce
    return jax.shard_map(
        make_per_device(reduce_grad),
        mesh=mesh,
        in_specs=placed,
        out_specs=(
            P(("fsdp", "dp"), None),
            P(("fsdp", "dp"), None),
            P("fsdp", None),
            P("fsdp", None),
            P("fsdp", None),
            P("fsdp", None),
            P("fsdp"),
            P("fsdp"),
            P(),
        ),
        check_vma=False,
    )
```

profile of v0, /device:TPU:0, one launch (start us, length us, event | category | flops | bytes accessed | tf_op | source)
XLA Modules:
  0.0 639.2 jit_solution(1268586833503978225)
XLA Ops:
  12.9 10.4 %all-gather = bf16[8,1,128]{2,1,0:T(2,128)(2,1)S(1)} all-gather(bf16[1,1,128]{2,1,0:T(2,128)(2,1)} %bitcast.194), channel_id=1, replica_groups=mesh['fsdp'=8,'dp'=4] {'fsdp'}, dimensions={0}, use_global_device_ids=true | all-gather | bytes 2304 | tf_op jit(solution)/shard_map/all_gather | solution.py:135
  23.3 8.8 %all-gather.1 = bf16[8,1,128]{2,1,0:T(2,128)(2,1)S(1)} all-gather(bf16[1,1,128]{2,1,0:T(2,128)(2,1)} %bitcast.195), channel_id=1, replica_groups=mesh['fsdp'=8,'dp'=4] {'fsdp'}, dimensions={0}, use_global_device_ids=true | all-gather | bytes 2304 | tf_op jit(solution)/shard_map/all_gather | solution.py:140
  32.9 7.8 %multiply_reduce_fusion.7 = (f32[512]{0:T(512)S(1)}, f32[512,1024]{1,0:T(8,128)S(1)}) fusion(bf16[4096,1024]{1,0:T(8,128)(2,1)} %param.11, s32[512]{0:T(512)} %param.14), kind=kOutput, calls=%fused_computation.64 | convolution fusion | flops 4298112512 | bytes 10489856 | tf_op jit(solution)/shard_map/dot_general | solution.py:147
  41.4 9.3 %fusion.12 = f32[512,1024]{1,0:T(8,128)} fusion(bf16[4096,1024]{1,0:T(8,128)(2,1)} %param.12, s32[512]{0:T(512)S(1)} %copy-done.15), kind=kOutput, calls=%fused_computation.28 | convolution fusion | flops 4297064448 | bytes 10487808 | tf_op jit(solution)/shard_map/dot_general | solution.py:181
  50.7 7.4 %all-gather.7.cloned.1.call-done = bf16[1024,3072]{1,0:T(8,128)(2,1)} async-done(((bf16[128,3072]{1,0:T(8,128)(2,1)}), bf16[1024,3072]{1,0:T(8,128)(2,1)}) %all-gather.7.cloned.1.call-update) | async-done | bytes 6291472 | tf_op jit(solution)/shard_map/all_gather | solution.py:134
  58.0 6.6 %convolution_convert_fusion = bf16[512,3072]{1,0:T(8,128)(2,1)S(1)} fusion(bf16[1024,3072]{1,0:T(8,128)(2,1)} %all-gather.7.cloned.1.call-done, f32[512,1024]{1,0:T(8,128)S(1)} %get-tuple-element.59, f32[1024]{0:T(1024)S(1)} %bitcast.180, f32[512]{0:T(512)S(1)} %fusion.84), kind=kOutput, calls=%fused_computation.34 | convolution fusion | flops 3224371200 | bytes 11540480 | tf_op jit(solution)/shard_map/dot_general | solution.py:153
  72.4 8.8 %fusion.1 = (f32[16,512]{1,0:T(8,128)S(1)}, f32[16,512,512]{1,2,0:T(8,128)}) fusion(pred[512,512]{0,1:T(8,128)(4,1)S(1)} %compare_and_fusion, bf16[512,16,64]{0,2,1:T(8,128)(2,1)} %bitcast.161, bf16[512,16,64]{0,2,1:T(8,128)(2,1)S(1)} %bitcast.159), kind=kOutput, calls=%fused_computation.11 | convolution fusion | flops 549445632 | bytes 19169280 | tf_op jit(solution)/shard_map/qhd,khd->hqk/dot_general | solution.py:29
  81.3 9.3 %fusion = f32[16,512]{1,0:T(8,128)S(1)} fusion(f32[16,512,512]{1,2,0:T(8,128)} %get-tuple-element.61, f32[16,512]{1,0:T(8,128)S(1)} %get-tuple-element.60, pred[512,512]{0,1:T(8,128)(4,1)S(1)} %compare_and_fusion), kind=kLoop, calls=%fused_computation.8 | loop fusion | flops 16769024 | bytes 17104896 | tf_op jit(solution)/shard_map/reduce_sum | solution.py:160
  90.6 9.5 %fusion.26 = bf16[16,64,512]{2,1,0:T(8,128)(2,1)} fusion(bf16[512,16,64]{0,2,1:T(8,128)(2,1)} %bitcast.175, f32[16,512,512]{1,2,0:T(8,128)} %get-tuple-element.61, f32[16,512]{1,0:T(8,128)S(1)} %fusion, f32[16,512]{1,0:T(8,128)S(1)} %get-tuple-element.60, pred[512,512]{0,1:T(8,128)(4,1)S(1)} %compare_and_fusion), kind=kOutput, calls=%fused_computation.68 | convolution fusion | flops 558366720 | bytes 19202048 | tf_op jit(solution)/shard_map/hqk,khd->qhd/dot_general | solution.py:163
  105.3 38.6 %all-gather.11.cloned.1.call-done = bf16[1024,4096]{1,0:T(8,128)(2,1)} async-done(((bf16[128,4096]{1,0:T(8,128)(2,1)}), bf16[1024,4096]{1,0:T(8,128)(2,1)}) %all-gather.11.cloned.1.call-update) | async-done | bytes 8388624 | tf_op jit(solution)/shard_map/all_gather | solution.py:139
  143.9 7.8 %fusion.96 = f32[512,4096]{1,0:T(8,128)S(1)} fusion(bf16[1024,4096]{1,0:T(8,128)(2,1)} %all-gather.11.cloned.1.call-done, f32[512,1024]{1,0:T(8,128)} %get-tuple-element.18, f32[1024]{0:T(1024)S(1)} %bitcast.184, f32[512]{0:T(512)S(1)} %fusion.85), kind=kOutput, calls=%fused_computation.181 | convolution fusion | flops 4296540160 | bytes 18880512 | tf_op jit(solution)/shard_map/dot_general | solution.py:171
  155.4 9.2 %fusion.93 = f32[4096,1024]{1,0:T(8,128)} fusion(f32[512,1024]{1,0:T(8,128)S(1)} %copy-done.40, f32[512]{0:T(512)S(1)} %bitcast.189, f32[512,4096]{1,0:T(8,128)S(1)} %fusion.96), kind=kOutput, calls=%fused_computation.178 | convolution fusion | flops 4314890240 | bytes 27265024 | tf_op jit(solution)/shard_map/kf,kd->fd/dot_general | solution.py:185
  164.7 35.3 %all-gather.13.cloned.1.call-done = bf16[4096,1024]{1,0:T(8,128)(2,1)} async-done(((bf16[512,1024]{1,0:T(8,128)(2,1)}), bf16[4096,1024]{1,0:T(8,128)(2,1)}) %all-gather.13.cloned.1.call-update) | async-done | bytes 8388624 | tf_op jit(solution)/shard_map/all_gather | solution.py:142
  199.9 13.3 %fusion.8 = bf16[512,4096]{1,0:T(8,128)(2,1)S(1)} fusion(f32[512,4096]{1,0:T(8,128)} %copy-done.39, bf16[4096,1024]{1,0:T(8,128)(2,1)} %all-gather.13.cloned.1.call-done, f32[512,1024]{1,0:T(8,128)} %fusion.12, f32[512]{0:T(512)S(1)} %bitcast.190), kind=kOutput, calls=%fused_computation.18 | convolution fusion | flops 4337958912 | bytes 23070720 | tf_op jit(solution)/shard_map/kd,fd->kf/dot_general | solution.py:189
  215.3 8.4 %fusion.95 = f32[1024,4096]{1,0:T(8,128)} fusion(bf16[512,4096]{1,0:T(8,128)(2,1)S(1)} %fusion.8, f32[512,1024]{1,0:T(8,128)S(1)} %copy-done.4, f32[1024]{0:T(1024)S(1)} %bitcast.185, f32[512]{0:T(512)S(1)} %fusion.85), kind=kOutput, calls=%fused_computation.180 | convolution fusion | flops 4296540160 | bytes 23074816 | tf_op jit(solution)/shard_map/kd,kf->df/dot_general | solution.py:194
  223.7 11.5 %multiply_reduce_fusion.1 = (f32[1024]{0:T(1024)}, f32[512]{0:T(512)S(1)}, f32[512,1024]{1,0:T(8,128)}) fusion(f32[512,1024]{1,0:T(8,128)S(1)} %copy-done.4, f32[512]{0:T(512)S(1)} %fusion.85, f32[1024]{0:T(1024)S(1)} %bitcast.186, bf16[512,4096]{1,0:T(8,128)(2,1)} %copy-done.38, bf16[1024,4096]{1,0:T(8,128)(2,1)} %all-gather.11.cloned.1.call-done), kind=kOutput, calls=%fused_computation.49 | convolution fusion | flops 4298111488 | bytes 16789504 | tf_op jit(solution)/shard_map/kf,df->kd/dot_general | solution.py:198
  235.3 10.3 %multiply_reduce_fusion.3 = (f32[512]{0:T(512)S(1)}, bf16[512,1024]{1,0:T(8,128)(2,1)S(1)}, f32[512,1024]{1,0:T(8,128)}) fusion(f32[512,1024]{1,0:T(8,128)S(1)} %copy-done.41, f32[512,1024]{1,0:T(8,128)S(1)} %copy-done.4, f32[512]{0:T(512)S(1)} %multiply_multiply_fusion.3, f32[512]{0:T(512)S(1)} %fusion.85, f32[512,1024]{1,0:T(8,128)} %get-tuple-element.63, ...), kind=kOutput, calls=%fused_computation.54 | convolution fusion | flops 4319608320 | bytes 28323840 | tf_op jit(solution)/shard_map/dot_general | solution.py:174
  251.2 11.5 %fusion.27 = bf16[16,64,512]{2,1,0:T(8,128)(2,1)} fusion(bf16[512,16,64]{0,2,1:T(8,128)(2,1)} %bitcast.177, f32[16,512]{1,0:T(8,128)S(1)} %log_add_fusion, f32[16,512,512]{1,2,0:T(8,128)} %get-tuple-element.61, pred[512,512]{0,1:T(8,128)(4,1)S(1)} %compare_and_fusion), kind=kOutput, calls=%fused_computation.70 | convolution fusion | flops 558366720 | bytes 19169280 | tf_op jit(solution)/shard_map/hqk,qhd->khd/dot_general | solution.py:227
  262.8 12.5 %multiply_reduce_fusion = (f32[16,512]{1,0:T(8,128)S(1)}, f32[16,512,512]{1,2,0:T(8,128)}) fusion(f32[16,512]{1,0:T(8,128)S(1)} %log_add_fusion, f32[16,512,512]{1,2,0:T(8,128)} %get-tuple-element.61, pred[512,512]{0,1:T(8,128)(4,1)S(1)} %compare_and_fusion, bf16[512,16,64]{0,2,1:T(8,128)(2,1)S(1)} %bitcast.178, bf16[512,16,64]{0,2,1:T(8,128)(2,1)S(1)} %bitcast.176), kind=kOutput, calls=%fused_computation.2 | convolution fusion | flops 562028544 | bytes 35979264 | tf_op jit(solution)/shard_map/qhd,khd->hqk/dot_general | solution.py:213
  275.2 12.6 %multiply_convert_fusion = bf16[16,512,512]{1,2,0:T(8,128)(2,1)S(1)} fusion(f32[16,512,512]{1,2,0:T(8,128)} %get-tuple-element.66, f32[16,512]{1,0:T(8,128)S(1)} %get-tuple-element.65, f32[16,512]{1,0:T(8,128)S(1)} %log_add_fusion, f32[16,512,512]{1,2,0:T(8,128)} %get-tuple-element.61, pred[512,512]{0,1:T(8,128)(4,1)S(1)} %compare_and_fusion), kind=kLoop, calls=%fused_computation.1 | loop fusion | flops 29360128 | bytes 42270720 | tf_op jit(solution)/shard_map/convert_element_type | solution.py:217
  293.8 6.0 fusion.17
  307.4 6.0 fusion.16
  313.7 9.0 %multiply_reduce_fusion.2 = (f32[1024]{0:T(1024)}, f32[512]{0:T(512)S(1)}, f32[512,1024]{1,0:T(8,128)}) fusion(f32[512,1024]{1,0:T(8,128)S(1)} %get-tuple-element.59, f32[512]{0:T(512)S(1)} %copy-done.34, f32[1024]{0:T(1024)S(1)} %bitcast.182, bf16[1024,3072]{1,0:T(8,128)(2,1)} %all-gather.7.cloned.1.call-done, bf16[512,1024]{0,1:T(8,128)(2,1)} %bitcast.201, ...), kind=kOutput, calls=%fused_computation.50 | convolution fusion | flops 3233806848 | bytes 13643776 | tf_op jit(solution)/shard_map/ke,de->kd/dot_general | solution.py:240
  346.4 52.0 %psum.39 = f32[3072]{0:T(1024)} all-reduce(f32[3072]{0:T(1024)S(1)} %pad_maximum_fusion.15), channel_id=1, replica_groups=mesh['fsdp'=8,'dp'=4] {'fsdp','dp'}, use_global_device_ids=true, to_apply=%region_16.17 | all-reduce | flops 3072 | bytes 24576 | tf_op jit(solution)/shard_map/psum | solution.py:250
  419.7 10.3 %bitcast_add_fusion = f32[4,512,1024]{2,1,0:T(8,128)} fusion(bf16[4,512,1024]{2,1,0:T(8,128)(2,1)} %collective-permute-done.15, f32[4,2,512,1024]{3,2,1,0:T(8,128)} %bitcast.164, s32[]{:T(128)S(6)} %select_n.97), kind=kLoop, calls=%fused_computation.21 | loop fusion | flops 4194304 | bytes 20971524 | tf_op jit(solution)/shard_map/add | solution.py:81
  440.2 19.6 %collective-permute-done.18 = bf16[2,256,1024]{2,1,0:T(8,128)(2,1)S(1)} collective-permute-done((bf16[2,256,1024]{2,1,0:T(8,128)(2,1)S(1)}, bf16[2,256,1024]{2,1,0:T(8,128)(2,1)S(1)}, u32[]{:S(2)}, u32[]{:S(2)}) %collective-permute-start.18) | collective-permute-done | bytes 1048608 | tf_op jit(solution)/shard_map/ppermute | solution.py:93
  463.5 18.8 %collective-permute-done.13 = bf16[2,64,4096]{2,1,0:T(8,128)(2,1)S(1)} collective-permute-done((bf16[2,64,4096]{2,1,0:T(8,128)(2,1)S(1)}, bf16[2,64,4096]{2,1,0:T(8,128)(2,1)S(1)}, u32[]{:S(2)}, u32[]{:S(2)}) %collective-permute-start.13) | collective-permute-done | bytes 1048608 | tf_op jit(solution)/shard_map/ppermute | solution.py:93
  486.8 6.7 %collective-permute-done.17 = bf16[256,1024]{1,0:T(8,128)(2,1)S(1)} collective-permute-done((bf16[256,1024]{1,0:T(8,128)(2,1)S(1)}, bf16[256,1024]{1,0:T(8,128)(2,1)S(1)}, u32[]{:S(2)}, u32[]{:S(2)}) %collective-permute-start.17) | collective-permute-done | bytes 524320 | tf_op jit(solution)/shard_map/ppermute | solution.py:100
  495.8 5.9 collective-permute-done.12
  504.3 10.0 %add_convert_fusion.1 = bf16[4096,1024]{1,0:T(8,128)(2,1)} fusion(bf16[4096,1024]{1,0:T(8,128)(2,1)} %param.11, s32[512]{0:T(512)S(1)} %copy-done.16, f32[512,1024]{1,0:T(8,128)} %get-tuple-element.64, f32[512]{0:T(512)S(1)} %bitcast.192), kind=kOutput, calls=%fused_computation.4 | convolution fusion | flops 4310695936 | bytes 18878464 | tf_op jit(solution)/shard_map/kt,kd->td/dot_general | solution.py:179
  514.4 11.7 %add_convert_fusion = bf16[4096,1024]{1,0:T(8,128)(2,1)} fusion(bf16[4096,1024]{1,0:T(8,128)(2,1)} %param.12, s32[512]{0:T(512)S(1)} %copy-done.16, f32[512,1024]{1,0:T(8,128)S(1)} %get-tuple-element.59, f32[512,1024]{1,0:T(8,128)S(1)} %copy-done.42, f32[1024]{0:T(1024)S(1)} %copy-done.19, f32[512]{0:T(512)S(1)} %copy-done.29, f32[512]{0:T(512)S(1)} %copy-done.32, ...), kind=kOutput, calls=%fused_computation | convolution fusion | flops 4316987392 | bytes 25190400 | tf_op jit(solution)/shard_map/kt,kd->td/dot_general | solution.py:247
  526.0 97.5 %all-reduce.3.cloned.1.call-done = (bf16[128,3072]{1,0:T(8,128)(2,1)}, bf16[128,1024]{1,0:T(8,128)(2,1)}, bf16[128,4096]{1,0:T(8,128)(2,1)}, bf16[512,1024]{1,0:T(8,128)(2,1)}) async-done(((bf16[128,3072]{1,0:T(8,128)(2,1)}, bf16[128,1024]{1,0:T(8,128)(2,1)}, bf16[128,4096]{1,0:T(8,128)(2,1)}, bf16[512,1024]{1,0:T(8,128)(2,1)}), (bf16[128,3072]{1,0:T(8,128)(2,1)}, bf16[128,1024]{1,0:T(8,128)(2,1)}, ...) | async-done | bytes 3145744 | tf_op jit(solution)/shard_map/psum | solution.py:107
  (222 shorter events, 121.6 us)
Async XLA Ops:
  7.2 50.9 %all-gather.7.cloned.1.call-start = ((), (), s32[]{:S(2)}) async-start(), calls=%async_computation | async-start | bytes 7077888 | tf_op jit(solution)/shard_map/all_gather | solution.py:134
  7.9 92.2 %all-gather.9.cloned.1.call-start = ((), (), s32[]{:S(2)}) async-start(), calls=%async_computation.1 | async-start | bytes 2359296 | tf_op jit(solution)/shard_map/all_gather | solution.py:137
  8.7 135.2 %all-gather.11.cloned.1.call-start = ((), (), s32[]{:S(2)}) async-start(), calls=%async_computation.2 | async-start | bytes 9437184 | tf_op jit(solution)/shard_map/all_gather | solution.py:139
  9.4 190.5 %all-gather.13.cloned.1.call-start = ((), (), s32[]{:S(2)}) async-start(), calls=%async_computation.3 | async-start | bytes 9437184 | tf_op jit(solution)/shard_map/all_gather | solution.py:142
  10.0 613.6 %all-reduce.3.cloned.1.call-start = ((), (), s32[]{:S(2)}) async-start(), calls=%async_computation.4 | async-start | bytes 6291456 | tf_op jit(solution)/shard_map/psum | solution.py:107
  23.3 34.8 %copy-start.20 = (f32[8,1,128]{2,1,0:T(1,128)}, f32[8,1,128]{2,1,0:T(1,128)S(1)}, u32[]{:S(2)}) copy-start(f32[8,1,128]{2,1,0:T(1,128)S(1)} %convert_element_type.306) | copy-start | bytes 12292
  32.1 203.1 %copy-start.22 = (f32[8,1,128]{2,1,0:T(1,128)}, f32[8,1,128]{2,1,0:T(1,128)S(1)}, u32[]{:S(2)}) copy-start(f32[8,1,128]{2,1,0:T(1,128)S(1)} %convert_element_type.307) | copy-start | bytes 12292
  41.4 193.8 %copy-start.26 = (f32[1,512]{1,0:T(1,128)}, f32[1,512]{1,0:T(1,128)S(1)}, u32[]{:S(2)}) copy-start(f32[1,512]{1,0:T(1,128)S(1)} %fusion.58) | copy-start | bytes 6148
  105.3 129.9 %copy-start.36 = (f32[512]{0:T(512)}, f32[512]{0:T(512)S(1)}, u32[]{:S(2)}) copy-start(f32[512]{0:T(512)S(1)} %fusion.85) | copy-start | bytes 6148
  245.6 80.9 %copy-start.28 = (f32[512]{0:T(512)}, f32[512]{0:T(512)S(1)}, u32[]{:S(2)}) copy-start(f32[512]{0:T(512)S(1)} %get-tuple-element.46) | copy-start | bytes 6148
  293.4 29.2 %collective-permute-start.5 = (bf16[4,128,1024]{2,1,0:T(8,128)(2,1)S(1)}, bf16[4,128,1024]{2,1,0:T(8,128)(2,1)}, u32[]{:S(2)}, u32[]{:S(2)}) collective-permute-start(bf16[4,128,1024]{2,1,0:T(8,128)(2,1)S(1)} %fusion.32), channel_id=1, source_target_pairs={{0,4},{4,0},{8,12},{12,8},{16,20},{20,16},{24,28},{28,24},{1,5},{5... | collective-permute-start | bytes 3145736 | tf_op jit(solution)/shard_map/ppermute | solution.py:80
  299.8 119.9 %collective-permute-start.15 = (bf16[4,512,1024]{2,1,0:T(8,128)(2,1)}, bf16[4,512,1024]{2,1,0:T(8,128)(2,1)}, u32[]{:S(2)}, u32[]{:S(2)}) collective-permute-start(bf16[4,512,1024]{2,1,0:T(8,128)(2,1)} %fusion.17), channel_id=1, source_target_pairs={{0,4},{4,0},{8,12},{12,8},{16,20},{20,16},{24,28},{28,24},{1,5},{5... | collective-permute-start | bytes 12582920 | tf_op jit(solution)/shard_map/ppermute | solution.py:80
  307.1 27.8 %collective-permute-start = (bf16[4,128,3072]{2,1,0:T(8,128)(2,1)}, bf16[4,128,3072]{2,1,0:T(8,128)(2,1)}, u32[]{:S(2)}, u32[]{:S(2)}) collective-permute-start(bf16[4,128,3072]{2,1,0:T(8,128)(2,1)} %fusion.22), channel_id=1, source_target_pairs={{0,4},{4,0},{8,12},{12,8},{16,20},{20,16},{24,28},{28,24},{1,5},{5... | collective-permute-start | bytes 9437192 | tf_op jit(solution)/shard_map/ppermute | solution.py:80
  313.4 98.5 %collective-permute-start.10 = (bf16[4,128,4096]{2,1,0:T(8,128)(2,1)}, bf16[4,128,4096]{2,1,0:T(8,128)(2,1)}, u32[]{:S(2)}, u32[]{:S(2)}) collective-permute-start(bf16[4,128,4096]{2,1,0:T(8,128)(2,1)} %fusion.16), channel_id=1, source_target_pairs={{0,4},{4,0},{8,12},{12,8},{16,20},{20,16},{24,28},{28,24},{1,5},{5... | collective-permute-start | bytes 12582920 | tf_op jit(solution)/shard_map/ppermute | solution.py:80
  324.4 8.5 %collective-permute-start.8 = (bf16[2,64,1024]{2,1,0:T(8,128)(2,1)S(1)}, bf16[2,64,1024]{2,1,0:T(8,128)(2,1)S(1)}, u32[]{:S(2)}, u32[]{:S(2)}) collective-permute-start(bf16[2,64,1024]{2,1,0:T(8,128)(2,1)S(1)} %pad_maximum_fusion.13), channel_id=1, source_target_pairs={{0,16},{4,20},{8,24},{12,28},{16,0},{20,4},{24,8},{28,12},{1,17},{... | collective-permute-start | bytes 786440 | tf_op jit(solution)/shard_map/ppermute | solution.py:93
  325.6 8.2 %collective-permute-start.6 = (bf16[2,64,1024]{2,1,0:T(8,128)(2,1)S(1)}, bf16[2,64,1024]{2,1,0:T(8,128)(2,1)S(1)}, u32[]{:S(2)}, u32[]{:S(2)}) collective-permute-start(bf16[2,64,1024]{2,1,0:T(8,128)(2,1)S(1)} %pad_maximum_fusion.12), channel_id=1, source_target_pairs={{0,8},{4,12},{8,0},{12,4},{16,24},{20,28},{24,16},{28,20},{1,9},{5... | collective-permute-start | bytes 786440 | tf_op jit(solution)/shard_map/ppermute | solution.py:90
  334.0 11.3 %collective-permute-start.7 = (bf16[64,1024]{1,0:T(8,128)(2,1)S(1)}, bf16[64,1024]{1,0:T(8,128)(2,1)S(1)}, u32[]{:S(2)}, u32[]{:S(2)}) collective-permute-start(bf16[64,1024]{1,0:T(8,128)(2,1)S(1)} %get-tuple-element.42), channel_id=1, source_target_pairs={{0,16},{4,20},{8,24},{12,28},{16,0},{20,4},{24,8},{28,12},{1,17},{... | collective-permute-start | bytes 393224 | tf_op jit(solution)/shard_map/ppermute | solution.py:100
  341.7 61.2 %collective-permute-start.3 = (bf16[2,64,3072]{2,1,0:T(8,128)(2,1)}, bf16[2,64,3072]{2,1,0:T(8,128)(2,1)}, u32[]{:S(2)}, u32[]{:S(2)}) collective-permute-start(bf16[2,64,3072]{2,1,0:T(8,128)(2,1)} %pad_maximum_fusion.10), channel_id=1, source_target_pairs={{0,16},{4,20},{8,24},{12,28},{16,0},{20,4},{24,8},{28,12},{1,17},{... | collective-permute-start | bytes 2359304 | tf_op jit(solution)/shard_map/ppermute | solution.py:93
  343.8 60.4 %collective-permute-start.1 = (bf16[2,64,3072]{2,1,0:T(8,128)(2,1)}, bf16[2,64,3072]{2,1,0:T(8,128)(2,1)}, u32[]{:S(2)}, u32[]{:S(2)}) collective-permute-start(bf16[2,64,3072]{2,1,0:T(8,128)(2,1)} %pad_maximum_fusion.9), channel_id=1, source_target_pairs={{0,8},{4,12},{8,0},{12,4},{16,24},{20,28},{24,16},{28,20},{1,9},{5... | collective-permute-start | bytes 2359304 | tf_op jit(solution)/shard_map/ppermute | solution.py:90
  345.3 55.7 %collective-permute-start.9 = (bf16[64,1024]{1,0:T(8,128)(2,1)S(1)}, bf16[64,1024]{1,0:T(8,128)(2,1)S(1)}, u32[]{:S(2)}, u32[]{:S(2)}) collective-permute-start(bf16[64,1024]{1,0:T(8,128)(2,1)S(1)} %get-tuple-element.43), channel_id=1, source_target_pairs={{0,8},{4,12},{8,0},{12,4},{16,24},{20,28},{24,16},{28,20},{1,9},{5... | collective-permute-start | bytes 393224 | tf_op jit(solution)/shard_map/ppermute | solution.py:103
  408.0 29.2 %collective-permute-start.2 = (bf16[64,3072]{1,0:T(8,128)(2,1)}, bf16[64,3072]{1,0:T(8,128)(2,1)S(1)}, u32[]{:S(2)}, u32[]{:S(2)}) collective-permute-start(bf16[64,3072]{1,0:T(8,128)(2,1)} %get-tuple-element.33), channel_id=1, source_target_pairs={{0,16},{4,20},{8,24},{12,28},{16,0},{20,4},{24,8},{28,12},{1,17},{... | collective-permute-start | bytes 1179656 | tf_op jit(solution)/shard_map/ppermute | solution.py:100
  410.7 27.8 %collective-permute-start.4 = (bf16[64,3072]{1,0:T(8,128)(2,1)}, bf16[64,3072]{1,0:T(8,128)(2,1)}, u32[]{:S(2)}, u32[]{:S(2)}) collective-permute-start(bf16[64,3072]{1,0:T(8,128)(2,1)} %get-tuple-element.34), channel_id=1, source_target_pairs={{0,8},{4,12},{8,0},{12,4},{16,24},{20,28},{24,16},{28,20},{1,9},{5... | collective-permute-start | bytes 1179656 | tf_op jit(solution)/shard_map/ppermute | solution.py:103
  433.7 26.1 %collective-permute-start.18 = (bf16[2,256,1024]{2,1,0:T(8,128)(2,1)S(1)}, bf16[2,256,1024]{2,1,0:T(8,128)(2,1)S(1)}, u32[]{:S(2)}, u32[]{:S(2)}) collective-permute-start(bf16[2,256,1024]{2,1,0:T(8,128)(2,1)S(1)} %pad_maximum_fusion.7), channel_id=1, source_target_pairs={{0,16},{4,20},{8,24},{12,28},{16,0},{20,4},{24,8},{28,12},{1,17},{... | collective-permute-start | bytes 3145736 | tf_op jit(solution)/shard_map/ppermute | solution.py:93
  434.3 26.1 %collective-permute-start.16 = (bf16[2,256,1024]{2,1,0:T(8,128)(2,1)S(1)}, bf16[2,256,1024]{2,1,0:T(8,128)(2,1)S(1)}, u32[]{:S(2)}, u32[]{:S(2)}) collective-permute-start(bf16[2,256,1024]{2,1,0:T(8,128)(2,1)S(1)} %pad_maximum_fusion.6), channel_id=1, source_target_pairs={{0,8},{4,12},{8,0},{12,4},{16,24},{20,28},{24,16},{28,20},{1,9},{5... | collective-permute-start | bytes 3145736 | tf_op jit(solution)/shard_map/ppermute | solution.py:90
  434.9 25.7 %slice-start = ((s8[8388608]{0:T(1024)(128)(4,1)}), s8[4194304]{0:T(1024)(128)(4,1)S(1)}, s32[]{:S(2)}) async-start(s8[8388608]{0:T(1024)(128)(4,1)} %bitcast.157), calls=%async_computation.5 | async-start | bytes 8388608
  435.0 47.3 %collective-permute-start.13 = (bf16[2,64,4096]{2,1,0:T(8,128)(2,1)S(1)}, bf16[2,64,4096]{2,1,0:T(8,128)(2,1)S(1)}, u32[]{:S(2)}, u32[]{:S(2)}) collective-permute-start(bf16[2,64,4096]{2,1,0:T(8,128)(2,1)S(1)} %pad_maximum_fusion.4), channel_id=1, source_target_pairs={{0,16},{4,20},{8,24},{12,28},{16,0},{20,4},{24,8},{28,12},{1,17},{... | collective-permute-start | bytes 3145736 | tf_op jit(solution)/shard_map/ppermute | solution.py:93
  437.2 23.4 %slice-start.1 = ((s8[8388608]{0:T(1024)(128)(4,1)}), s8[4194304]{0:T(1024)(128)(4,1)S(1)}, s32[]{:S(2)}) async-start(s8[8388608]{0:T(1024)(128)(4,1)} %bitcast.157), calls=%async_computation.6 | async-start | bytes 8388608
  437.2 45.6 %collective-permute-start.11 = (bf16[2,64,4096]{2,1,0:T(8,128)(2,1)S(1)}, bf16[2,64,4096]{2,1,0:T(8,128)(2,1)S(1)}, u32[]{:S(2)}, u32[]{:S(2)}) collective-permute-start(bf16[2,64,4096]{2,1,0:T(8,128)(2,1)S(1)} %pad_maximum_fusion.3), channel_id=1, source_target_pairs={{0,8},{4,12},{8,0},{12,4},{16,24},{20,28},{24,16},{28,20},{1,9},{5... | collective-permute-start | bytes 3145736 | tf_op jit(solution)/shard_map/ppermute | solution.py:90
  460.9 32.6 %collective-permute-start.17 = (bf16[256,1024]{1,0:T(8,128)(2,1)S(1)}, bf16[256,1024]{1,0:T(8,128)(2,1)S(1)}, u32[]{:S(2)}, u32[]{:S(2)}) collective-permute-start(bf16[256,1024]{1,0:T(8,128)(2,1)S(1)} %get-tuple-element.21), channel_id=1, source_target_pairs={{0,16},{4,20},{8,24},{12,28},{16,0},{20,4},{24,8},{28,12},{1,17},{... | collective-permute-start | bytes 1572872 | tf_op jit(solution)/shard_map/ppermute | solution.py:100
  462.6 31.4 %collective-permute-start.19 = (bf16[256,1024]{1,0:T(8,128)(2,1)S(1)}, bf16[256,1024]{1,0:T(8,128)(2,1)S(1)}, u32[]{:S(2)}, u32[]{:S(2)}) collective-permute-start(bf16[256,1024]{1,0:T(8,128)(2,1)S(1)} %get-tuple-element.22), channel_id=1, source_target_pairs={{0,8},{4,12},{8,0},{12,4},{16,24},{20,28},{24,16},{28,20},{1,9},{5... | collective-permute-start | bytes 1572872 | tf_op jit(solution)/shard_map/ppermute | solution.py:103
  483.3 18.3 %collective-permute-start.12 = (bf16[64,4096]{1,0:T(8,128)(2,1)S(1)}, bf16[64,4096]{1,0:T(8,128)(2,1)S(1)}, u32[]{:S(2)}, u32[]{:S(2)}) collective-permute-start(bf16[64,4096]{1,0:T(8,128)(2,1)S(1)} %get-tuple-element.27), channel_id=1, source_target_pairs={{0,16},{4,20},{8,24},{12,28},{16,0},{20,4},{24,8},{28,12},{1,17},{... | collective-permute-start | bytes 1572872 | tf_op jit(solution)/shard_map/ppermute | solution.py:100
  485.0 17.7 %collective-permute-start.14 = (bf16[64,4096]{1,0:T(8,128)(2,1)S(1)}, bf16[64,4096]{1,0:T(8,128)(2,1)S(1)}, u32[]{:S(2)}, u32[]{:S(2)}) collective-permute-start(bf16[64,4096]{1,0:T(8,128)(2,1)S(1)} %get-tuple-element.28), channel_id=1, source_target_pairs={{0,8},{4,12},{8,0},{12,4},{16,24},{20,28},{24,16},{28,20},{1,9},{5... | collective-permute-start | bytes 1572872 | tf_op jit(solution)/shard_map/ppermute | solution.py:103
  (41 other events, 360.2 us)
Sparse Core Ops, SparseCore 0:
  9.9 48.1 all-gather.6
  59.9 27.7 all-gather.8
  89.6 54.2 all-gather.10
  145.6 54.2 all-gather.12
  504.3 119.2 all-reduce.2
where the time goes:
time: 649 us; the launch traced here: 639 us
  waiting for transfers between devices  241 us (37%)
  matrix products  177 us (27%)
  other arithmetic  71.4 us (11%)
  blocking collectives  71.3 us (11%)
  local copies, waits for them, and re-layouts  43.3 us (7%)
  starting transfers between devices  20.8 us (3%)
  between operations  15.1 us (2%)
    psum x1, waiting for transfers between devices, plane_reduce(): return lax.psum(shard.astype(jnp.bfloat16), 'dp').astype(jnp.float32)  97.5 us
    psum x1, blocking collectives, per_device(): lax.psum(jnp.concatenate([grad_gain_one, grad_gain_two, router_local]), (...  52 us
    ppermute x4, waiting for transfers between devices, plane_reduce(): lax.ppermute(jnp.stack([to_y[half:], to_d[half:]]).astype(jnp.bfloat16),...  43.7 us
    all_gather x1, waiting for transfers between devices, per_device(): lax.all_gather(mlp_in, 'fsdp', axis=0, tiled=True)  38.6 us
    all_gather x1, waiting for transfers between devices, per_device(): w_down = lax.all_gather(mlp_out, 'fsdp', axis=0, tiled=True)  35.3 us
    add x4, other arithmetic, plane_reduce(): chip = keep + got.astype(jnp.float32)  20.5 us
    convert_element_type x4, local copies, waits for them, and re-layouts, plane_reduce(): got = lax.ppermute(send.astype(jnp.bfloat16), 'fsdp', swap_pairs(1, 8))  14.3 us
    dot_general x1, matrix products, per_device(): jnp.einsum('kd,fd->kf', grad_expanded, w_down, preferred_element_type=jnp...  13.3 us
  transfers between devices with their start and end apart: 25, of which 14 were waited for; matrix products, arithmetic and copies ran while one was open for 28% of the time, Pallas kernels for 0%

commit v1 on v0

--- a/solution.py
+++ b/solution.py
@@ -8,6 +8,27 @@
 HEAD = 64
 EPS = 1e-06
 MASKED = -1e30
+
+
+def collect(shard, axis, dim):
+    peers, index, rows = (lax.axis_size(axis), lax.axis_index(axis), shard.shape[dim])
+    forward = [(i, (i + 1) % peers) for i in range(peers)]
+    left = [(i, (i - 1) % peers) for i in range(peers)]
+    result = jnp.zeros((*shard.shape[:dim], peers * rows, *shard.shape[dim + 1 :]), shard.dtype)
+    result = lax.dynamic_update_slice_in_dim(result, shard, index * rows, axis=dim)
+    from_left = from_right = shard
+    half = peers // 2
+    for step in range(1, half + 1):
+        from_left = lax.ppermute(from_left, axis, forward)
+        result = lax.dynamic_update_slice_in_dim(
+            result, from_left, (index - step) % peers * rows, axis=dim
+        )
+        if step < peers - half:
+            from_right = lax.ppermute(from_right, axis, left)
+            result = lax.dynamic_update_slice_in_dim(
+                result, from_right, (index + step) % peers * rows, axis=dim
+            )
+    return result
 
 
 def rms_scale(values, gain_vec):
@@ -136,7 +157,7 @@
         )
         w_out = lax.all_gather(attn_out, "fsdp", axis=0, tiled=True)
         w_in, gain_mlp = (
-            lax.all_gather(mlp_in, "fsdp", axis=0, tiled=True),
+            collect(mlp_in, "fsdp", 0),
             lax.all_gather(norm_mlp, "fsdp", axis=0, tiled=True),
         )
         w_down = lax.all_gather(mlp_out, "fsdp", axis=0, tiled=True)

time: 649 us -> 662 us (1.020)
  waiting for transfers between devices: 241 us -> 222 us
  local copies, waits for them, and re-layouts: 43.3 us -> 59.1 us
  blocking collectives: 71.3 us -> 85 us
    ppermute x0 -> x7, waiting for transfers between devices: none -> 54 us  [the longest x4 52.6 us: collect(): from_left = lax.ppermute(from_left, axis, forward)]
    all_gather x1 -> x0, waiting for transfers between devices: 38.6 us -> none  [per_device(): lax.all_gather(mlp_in, 'fsdp', axis=0, tiled=True)]
    all_gather x1, waiting for transfers between devices: 35.3 us -> 0.02 us  [per_device(): w_down = lax.all_gather(mlp_out, 'fsdp', axis=0, tiled=True)]
    all_gather x1, blocking collectives: 10.4 us -> 36.3 us  [per_device(): lax.all_gather(norm_attn, 'fsdp', axis=0, tiled=True)]
    ppermute x4, waiting for transfers between devices: 12.6 us -> 27.9 us  [plane_reduce(): lax.ppermute(pass_a.astype(jnp.bfloat16), 'fsdp', swap_pairs(4, 8))]
    ppermute x4, waiting for transfers between devices: 43.7 us -> 29.8 us  [plane_reduce(): lax.ppermute(jnp.stack([to_y[half:], to_d[half:]]).astype(jnp.bfloat16),...]
    psum x1, blocking collectives: 52 us -> 39.7 us  [per_device(): lax.psum(jnp.concatenate([grad_gain_one, grad_gain_two, router_local]), (...]
    dynamic_update_slice x0 -> x8, local copies, waits for them, and re-layouts: none -> 12.1 us  [the longest x4 6.65 us: collect(): lax.dynamic_update_slice_in_dim(result, from_left, (index - step) % peers...]
  transfers between devices with their start and end apart: 25 -> 31, of which waited for: 14 -> 14; matrix products, arithmetic and copies ran while one was open for 28% -> 42% of each run, Pallas kernels for 0% -> 0%
where the time goes in v1:
time: 662 us; the launch traced here: 654 us
  waiting for transfers between devices  222 us (34%)
  matrix products  176 us (27%)
  blocking collectives  85 us (13%)
  other arithmetic  70.2 us (11%)
  local copies, waits for them, and re-layouts  59.1 us (9%)
  starting transfers between devices  26.6 us (4%)
  between operations  15.2 us (2%)
    psum x1, waiting for transfers between devices, plane_reduce(): return lax.psum(shard.astype(jnp.bfloat16), 'dp').astype(jnp.float32)  98.3 us
    ppermute x4, waiting for transfers between devices, collect(): from_left = lax.ppermute(from_left, axis, forward)  52.6 us
    psum x1, blocking collectives, per_device(): lax.psum(jnp.concatenate([grad_gain_one, grad_gain_two, router_local]), (...  39.7 us
    all_gather x1, blocking collectives, per_device(): lax.all_gather(norm_attn, 'fsdp', axis=0, tiled=True)  36.3 us
    ppermute x4, waiting for transfers between devices, plane_reduce(): lax.ppermute(jnp.stack([to_y[half:], to_d[half:]]).astype(jnp.bfloat16),...  29.8 us
    ppermute x4, waiting for transfers between devices, plane_reduce(): lax.ppermute(pass_a.astype(jnp.bfloat16), 'fsdp', swap_pairs(4, 8))  27.9 us
    unnamed x115, local copies, waits for them, and re-layouts  21.8 us
    add x4, other arithmetic, plane_reduce(): chip = keep + got.astype(jnp.float32)  18 us
  transfers between devices with their start and end apart: 31, of which 14 were waited for; matrix products, arithmetic and copies ran while one was open for 42% of the time, Pallas kernels for 0%

profile of v1, /device:TPU:0, one launch (start us, length us, event | category | flops | bytes accessed | tf_op | source)
XLA Modules:
  0.0 653.8 jit_solution(10631853594913414510)
XLA Ops:
  12.3 7.8 %multiply_reduce_fusion.7 = (f32[512]{0:T(512)S(1)}, f32[512,1024]{1,0:T(8,128)S(1)}) fusion(bf16[4096,1024]{1,0:T(8,128)(2,1)} %param.11, s32[512]{0:T(512)} %param.14), kind=kOutput, calls=%fused_computation.64 | convolution fusion | flops 4298112512 | bytes 10489856 | tf_op jit(solution)/shard_map/dot_general | solution.py:168
  20.3 9.5 %fusion.12 = f32[512,1024]{1,0:T(8,128)} fusion(bf16[4096,1024]{1,0:T(8,128)(2,1)} %param.12, s32[512]{0:T(512)S(1)} %copy-done.24), kind=kOutput, calls=%fused_computation.28 | convolution fusion | flops 4297064448 | bytes 10487808 | tf_op jit(solution)/shard_map/dot_general | solution.py:202
  29.9 12.1 %collective-permute-done = bf16[128,4096]{1,0:T(8,128)(2,1)} collective-permute-done((bf16[128,4096]{1,0:T(8,128)(2,1)}, bf16[128,4096]{1,0:T(8,128)(2,1)}, u32[]{:S(2)}, u32[]{:S(2)}) %collective-permute-start) | collective-permute-done | bytes 1048608 | tf_op jit(solution)/shard_map/ppermute | solution.py:22
  52.1 36.3 %all-gather = bf16[8,1,128]{2,1,0:T(2,128)(2,1)S(1)} all-gather(bf16[1,1,128]{2,1,0:T(2,128)(2,1)S(1)} %bitcast.194), channel_id=1, replica_groups=mesh['fsdp'=8,'dp'=4] {'fsdp'}, dimensions={0}, use_global_device_ids=true | all-gather | bytes 2304 | tf_op jit(solution)/shard_map/all_gather | solution.py:156
  88.4 9.0 %all-gather.1 = bf16[8,1,128]{2,1,0:T(2,128)(2,1)S(1)} all-gather(bf16[1,1,128]{2,1,0:T(2,128)(2,1)S(1)} %bitcast.195), channel_id=1, replica_groups=mesh['fsdp'=8,'dp'=4] {'fsdp'}, dimensions={0}, use_global_device_ids=true | all-gather | bytes 2304 | tf_op jit(solution)/shard_map/all_gather | solution.py:161
  106.9 19.1 %collective-permute-done.4 = bf16[128,4096]{1,0:T(8,128)(2,1)S(1)} collective-permute-done((bf16[128,4096]{1,0:T(8,128)(2,1)}, bf16[128,4096]{1,0:T(8,128)(2,1)S(1)}, u32[]{:S(2)}, u32[]{:S(2)}) %collective-permute-start.4) | collective-permute-done | bytes 1048608 | tf_op jit(solution)/shard_map/ppermute | solution.py:22
  130.7 21.4 %collective-permute-done.6 = bf16[128,4096]{1,0:T(8,128)(2,1)S(1)} collective-permute-done((bf16[128,4096]{1,0:T(8,128)(2,1)S(1)}, bf16[128,4096]{1,0:T(8,128)(2,1)S(1)}, u32[]{:S(2)}, u32[]{:S(2)}) %collective-permute-start.6) | collective-permute-done | bytes 1048608 | tf_op jit(solution)/shard_map/ppermute | solution.py:22
  153.1 6.6 %convolution_convert_fusion = bf16[512,3072]{1,0:T(8,128)(2,1)S(1)} fusion(bf16[1024,3072]{1,0:T(8,128)(2,1)} %all-gather.6.cloned.1.call-done, f32[512,1024]{1,0:T(8,128)S(1)} %get-tuple-element.59, f32[1024]{0:T(1024)S(1)} %bitcast.180, f32[512]{0:T(512)S(1)} %fusion.84), kind=kOutput, calls=%fused_computation.34 | convolution fusion | flops 3224371200 | bytes 11540480 | tf_op jit(solution)/shard_map/dot_general | solution.py:174
  166.5 8.6 %fusion.1 = (f32[16,512]{1,0:T(8,128)S(1)}, f32[16,512,512]{1,2,0:T(8,128)}) fusion(pred[512,512]{0,1:T(8,128)(4,1)S(1)} %compare_and_fusion, bf16[512,16,64]{0,2,1:T(8,128)(2,1)} %bitcast.161, bf16[512,16,64]{0,2,1:T(8,128)(2,1)S(1)} %bitcast.159), kind=kOutput, calls=%fused_computation.11 | convolution fusion | flops 549445632 | bytes 19169280 | tf_op jit(solution)/shard_map/qhd,khd->hqk/dot_general | solution.py:50
  175.1 9.3 %fusion = f32[16,512]{1,0:T(8,128)S(1)} fusion(f32[16,512,512]{1,2,0:T(8,128)} %get-tuple-element.61, f32[16,512]{1,0:T(8,128)S(1)} %get-tuple-element.60, pred[512,512]{0,1:T(8,128)(4,1)S(1)} %compare_and_fusion), kind=kLoop, calls=%fused_computation.8 | loop fusion | flops 16769024 | bytes 17104896 | tf_op jit(solution)/shard_map/reduce_sum | solution.py:181
  184.4 9.2 %fusion.26 = bf16[16,64,512]{2,1,0:T(8,128)(2,1)} fusion(bf16[512,16,64]{0,2,1:T(8,128)(2,1)} %bitcast.175, f32[16,512,512]{1,2,0:T(8,128)} %get-tuple-element.61, f32[16,512]{1,0:T(8,128)S(1)} %fusion, f32[16,512]{1,0:T(8,128)S(1)} %get-tuple-element.60, pred[512,512]{0,1:T(8,128)(4,1)S(1)} %compare_and_fusion), kind=kOutput, calls=%fused_computation.68 | convolution fusion | flops 558366720 | bytes 19202048 | tf_op jit(solution)/shard_map/hqk,khd->qhd/dot_general | solution.py:184
  198.2 11.7 %fusion.96 = f32[512,4096]{1,0:T(8,128)} fusion(bf16[1024,4096]{1,0:T(8,128)(2,1)} %constant_dynamic-update-slice_fusion, f32[512,1024]{1,0:T(8,128)S(1)} %get-tuple-element.18, f32[1024]{0:T(1024)S(1)} %bitcast.184, f32[512]{0:T(512)S(1)} %fusion.85), kind=kOutput, calls=%fused_computation.189 | convolution fusion | flops 4296540160 | bytes 18880512 | tf_op jit(solution)/shard_map/dot_general | solution.py:192
  209.8 8.2 %fusion.93 = f32[4096,1024]{1,0:T(8,128)S(1)} fusion(f32[512,1024]{1,0:T(8,128)S(1)} %copy-done.51, f32[512]{0:T(512)S(1)} %bitcast.189, f32[512,4096]{1,0:T(8,128)} %fusion.96), kind=kOutput, calls=%fused_computation.186 | convolution fusion | flops 4314890240 | bytes 27265024 | tf_op jit(solution)/shard_map/kf,kd->fd/dot_general | solution.py:206
  218.1 5.8 copy-done.6
  226.6 14.7 %fusion.8 = bf16[512,4096]{1,0:T(8,128)(2,1)} fusion(f32[512,4096]{1,0:T(8,128)} %fusion.96, bf16[4096,1024]{1,0:T(8,128)(2,1)} %all-gather.10.cloned.1.call-done, f32[512,1024]{1,0:T(8,128)} %fusion.12, f32[512]{0:T(512)S(1)} %bitcast.190), kind=kOutput, calls=%fused_computation.18 | convolution fusion | flops 4337958912 | bytes 23070720 | tf_op jit(solution)/shard_map/kd,fd->kf/dot_general | solution.py:210
  241.3 11.5 %multiply_reduce_fusion.1 = (f32[1024]{0:T(1024)}, f32[512]{0:T(512)S(1)}, f32[512,1024]{1,0:T(8,128)}) fusion(f32[512,1024]{1,0:T(8,128)S(1)} %copy-done.13, f32[512]{0:T(512)S(1)} %fusion.85, f32[1024]{0:T(1024)S(1)} %bitcast.185, bf16[512,4096]{1,0:T(8,128)(2,1)} %fusion.8, bf16[1024,4096]{1,0:T(8,128)(2,1)} %constant_dynamic-update-slice_fusion), kind=kOutput, calls=%fused_computation.49 | convolution fusion | flops 4298111488 | bytes 16789504 | tf_op jit(solution)/shard_map/kf,df->kd/dot_general | solution.py:219
  252.9 9.9 %multiply_reduce_fusion.3 = (f32[512]{0:T(512)S(1)}, bf16[512,1024]{1,0:T(8,128)(2,1)S(1)}, f32[512,1024]{1,0:T(8,128)}) fusion(f32[512,1024]{1,0:T(8,128)S(1)} %copy-done.52, f32[512,1024]{1,0:T(8,128)S(1)} %copy-done.13, f32[512]{0:T(512)S(1)} %multiply_multiply_fusion.3, f32[512]{0:T(512)S(1)} %fusion.85, f32[512,1024]{1,0:T(8,128)} %get-tuple-element.63, ...), kind=kOutput, calls=%fused_computation.54 | convolution fusion | flops 4319608320 | bytes 28323840 | tf_op jit(solution)/shard_map/dot_general | solution.py:195
  268.3 12.8 %multiply_reduce_fusion = (f32[16,512]{1,0:T(8,128)S(1)}, f32[16,512,512]{1,2,0:T(8,128)}) fusion(f32[16,512]{1,0:T(8,128)S(1)} %log_add_fusion, f32[16,512,512]{1,2,0:T(8,128)} %get-tuple-element.61, pred[512,512]{0,1:T(8,128)(4,1)S(1)} %compare_and_fusion, bf16[512,16,64]{0,2,1:T(8,128)(2,1)} %bitcast.177, bf16[512,16,64]{0,2,1:T(8,128)(2,1)} %bitcast.176), kind=kOutput, calls=%fused_computation.2 | convolution fusion | flops 562028544 | bytes 35979264 | tf_op jit(solution)/shard_map/qhd,khd->hqk/dot_general | solution.py:234
  281.1 12.3 %multiply_convert_fusion = bf16[16,512,512]{1,2,0:T(8,128)(2,1)S(1)} fusion(f32[16,512,512]{1,2,0:T(8,128)} %get-tuple-element.66, f32[16,512]{1,0:T(8,128)S(1)} %get-tuple-element.65, f32[16,512]{1,0:T(8,128)S(1)} %log_add_fusion, f32[16,512,512]{1,2,0:T(8,128)} %get-tuple-element.61, pred[512,512]{0,1:T(8,128)(4,1)S(1)} %compare_and_fusion), kind=kLoop, calls=%fused_computation.1 | loop fusion | flops 29360128 | bytes 42270720 | tf_op jit(solution)/shard_map/convert_element_type | solution.py:238
  298.5 7.1 %fusion.95 = f32[1024,4096]{1,0:T(8,128)S(1)} fusion(bf16[512,4096]{1,0:T(8,128)(2,1)} %fusion.8, f32[512,1024]{1,0:T(8,128)S(1)} %copy-done.14, f32[1024]{0:T(1024)S(1)} %bitcast.187, f32[512]{0:T(512)S(1)} %fusion.85), kind=kOutput, calls=%fused_computation.188 | convolution fusion | flops 4296540160 | bytes 23074816 | tf_op jit(solution)/shard_map/kd,kf->df/dot_general | solution.py:215
  314.9 10.4 %fusion.27 = bf16[16,64,512]{2,1,0:T(8,128)(2,1)S(1)} fusion(bf16[512,16,64]{0,2,1:T(8,128)(2,1)} %bitcast.178, f32[16,512]{1,0:T(8,128)S(1)} %log_add_fusion, f32[16,512,512]{1,2,0:T(8,128)} %get-tuple-element.61, pred[512,512]{0,1:T(8,128)(4,1)S(1)} %compare_and_fusion), kind=kOutput, calls=%fused_computation.70 | convolution fusion | flops 558366720 | bytes 19169280 | tf_op jit(solution)/shard_map/hqk,qhd->khd/dot_general | solution.py:248
  337.1 8.0 %multiply_reduce_fusion.2 = (f32[1024]{0:T(1024)S(1)}, f32[512]{0:T(512)S(1)}, f32[512,1024]{1,0:T(8,128)}) fusion(f32[512,1024]{1,0:T(8,128)S(1)} %get-tuple-element.59, f32[512]{0:T(512)S(1)} %copy-done.43, f32[1024]{0:T(1024)S(1)} %bitcast.182, bf16[1024,3072]{1,0:T(8,128)(2,1)} %all-gather.6.cloned.1.call-done, bf16[512,1024]{0,1:T(8,128)(2,1)S(1)} %bitcast.199, ...), kind=kOutput, calls=%fused_computation.50 | convolution fusion | flops 3233806848 | bytes 13643776 | tf_op jit(solution)/shard_map/ke,de->kd/dot_general | solution.py:261
  345.1 6.0 bitcast_add_fusion
  370.3 21.8 %collective-permute-done.14 = bf16[64,1024]{1,0:T(8,128)(2,1)S(1)} collective-permute-done((bf16[64,1024]{1,0:T(8,128)(2,1)S(1)}, bf16[64,1024]{1,0:T(8,128)(2,1)S(1)}, u32[]{:S(2)}, u32[]{:S(2)}) %collective-permute-start.14) | collective-permute-done | bytes 131104 | tf_op jit(solution)/shard_map/ppermute | solution.py:121
  392.6 39.7 %psum.39 = f32[3072]{0:T(1024)} all-reduce(f32[3072]{0:T(1024)S(1)} %pad_maximum_fusion.15), channel_id=1, replica_groups=mesh['fsdp'=8,'dp'=4] {'fsdp','dp'}, use_global_device_ids=true, to_apply=%region_16.17 | all-reduce | flops 3072 | bytes 24576 | tf_op jit(solution)/shard_map/psum | solution.py:271
  466.9 9.1 %collective-permute-done.10 = bf16[2,64,3072]{2,1,0:T(8,128)(2,1)} collective-permute-done((bf16[2,64,3072]{2,1,0:T(8,128)(2,1)S(1)}, bf16[2,64,3072]{2,1,0:T(8,128)(2,1)}, u32[]{:S(2)}, u32[]{:S(2)}) %collective-permute-start.10) | collective-permute-done | bytes 786464 | tf_op jit(solution)/shard_map/ppermute | solution.py:114
  482.1 16.2 %collective-permute-done.20 = bf16[2,64,4096]{2,1,0:T(8,128)(2,1)S(1)} collective-permute-done((bf16[2,64,4096]{2,1,0:T(8,128)(2,1)S(1)}, bf16[2,64,4096]{2,1,0:T(8,128)(2,1)S(1)}, u32[]{:S(2)}, u32[]{:S(2)}) %collective-permute-start.20) | collective-permute-done | bytes 1048608 | tf_op jit(solution)/shard_map/ppermute | solution.py:114
  502.5 6.3 collective-permute-done.11
  510.1 6.0 collective-permute-done.19
  519.2 10.0 %add_convert_fusion.1 = bf16[4096,1024]{1,0:T(8,128)(2,1)} fusion(bf16[4096,1024]{1,0:T(8,128)(2,1)} %param.11, s32[512]{0:T(512)S(1)} %copy-done.25, f32[512,1024]{1,0:T(8,128)} %get-tuple-element.64, f32[512]{0:T(512)S(1)} %bitcast.192), kind=kOutput, calls=%fused_computation.4 | convolution fusion | flops 4310695936 | bytes 18878464 | tf_op jit(solution)/shard_map/kt,kd->td/dot_general | solution.py:200
  529.3 11.6 %add_convert_fusion = bf16[4096,1024]{1,0:T(8,128)(2,1)} fusion(bf16[4096,1024]{1,0:T(8,128)(2,1)} %param.12, s32[512]{0:T(512)S(1)} %copy-done.25, f32[512,1024]{1,0:T(8,128)S(1)} %get-tuple-element.59, f32[512,1024]{1,0:T(8,128)S(1)} %copy-done.53, f32[1024]{0:T(1024)S(1)} %copy-done.29, f32[512]{0:T(512)S(1)} %copy-done.38, f32[512]{0:T(512)S(1)} %copy-done.41, ...), kind=kOutput, calls=%fused_computation | convolution fusion | flops 4316987392 | bytes 25190400 | tf_op jit(solution)/shard_map/kt,kd->td/dot_general | solution.py:268
  540.9 98.3 %all-reduce.3.cloned.1.call-done = (bf16[128,3072]{1,0:T(8,128)(2,1)}, bf16[128,1024]{1,0:T(8,128)(2,1)}, bf16[128,4096]{1,0:T(8,128)(2,1)}, bf16[512,1024]{1,0:T(8,128)(2,1)}) async-done(((bf16[128,3072]{1,0:T(8,128)(2,1)}, bf16[128,1024]{1,0:T(8,128)(2,1)}, bf16[128,4096]{1,0:T(8,128)(2,1)}, bf16[512,1024]{1,0:T(8,128)(2,1)}), (bf16[128,3072]{1,0:T(8,128)(2,1)}, bf16[128,1024]{1,0:T(8,128)(2,1)}, ...) | async-done | bytes 3145744 | tf_op jit(solution)/shard_map/psum | solution.py:128
  (259 shorter events, 152.1 us)
Async XLA Ops:
  7.2 145.9 %all-gather.6.cloned.1.call-start = ((), (), s32[]{:S(2)}) async-start(), calls=%async_computation | async-start | bytes 7077888 | tf_op jit(solution)/shard_map/all_gather | solution.py:155
  7.9 185.7 %all-gather.8.cloned.1.call-start = ((), (), s32[]{:S(2)}) async-start(), calls=%async_computation.1 | async-start | bytes 2359296 | tf_op jit(solution)/shard_map/all_gather | solution.py:158
  8.7 217.9 %all-gather.10.cloned.1.call-start = ((), (), s32[]{:S(2)}) async-start(), calls=%async_computation.2 | async-start | bytes 9437184 | tf_op jit(solution)/shard_map/all_gather | solution.py:163
  8.7 33.3 %collective-permute-start = (bf16[128,4096]{1,0:T(8,128)(2,1)}, bf16[128,4096]{1,0:T(8,128)(2,1)}, u32[]{:S(2)}, u32[]{:S(2)}) collective-permute-start(bf16[128,4096]{1,0:T(8,128)(2,1)} %param.17), channel_id=1, source_target_pairs={{0,4},{4,8},{8,12},{12,16},{16,20},{20,24},{24,28},{28,0},{1,5},{5... | collective-permute-start | bytes 3145736 | tf_op jit(solution)/shard_map/ppermute | solution.py:22
  9.3 39.9 %collective-permute-start.1 = (bf16[128,4096]{1,0:T(8,128)(2,1)}, bf16[128,4096]{1,0:T(8,128)(2,1)}, u32[]{:S(2)}, u32[]{:S(2)}) collective-permute-start(bf16[128,4096]{1,0:T(8,128)(2,1)} %param.17), channel_id=1, source_target_pairs={{0,28},{4,0},{8,4},{12,8},{16,12},{20,16},{24,20},{28,24},{1,29},{... | collective-permute-start | bytes 3145736 | tf_op jit(solution)/shard_map/ppermute | solution.py:27
  12.2 627.0 %all-reduce.3.cloned.1.call-start = ((), (), s32[]{:S(2)}) async-start(), calls=%async_computation.3 | async-start | bytes 6291456 | tf_op jit(solution)/shard_map/psum | solution.py:128
  42.0 55.4 %collective-permute-start.2 = (bf16[128,4096]{1,0:T(8,128)(2,1)}, bf16[128,4096]{1,0:T(8,128)(2,1)}, u32[]{:S(2)}, u32[]{:S(2)}) collective-permute-start(bf16[128,4096]{1,0:T(8,128)(2,1)} %collective-permute-done), channel_id=1, source_target_pairs={{0,4},{4,8},{8,12},{12,16},{16,20},{20,24},{24,28},{28,0},{1,5},{5... | collective-permute-start | bytes 3145736 | tf_op jit(solution)/shard_map/ppermute | solution.py:22
  43.2 209.6 %copy-start.35 = (f32[1,512]{1,0:T(1,128)}, f32[1,512]{1,0:T(1,128)S(1)}, u32[]{:S(2)}) copy-start(f32[1,512]{1,0:T(1,128)S(1)} %fusion.58) | copy-start | bytes 6148
  49.2 53.3 %collective-permute-start.3 = (bf16[128,4096]{1,0:T(8,128)(2,1)}, bf16[128,4096]{1,0:T(8,128)(2,1)S(1)}, u32[]{:S(2)}, u32[]{:S(2)}) collective-permute-start(bf16[128,4096]{1,0:T(8,128)(2,1)} %collective-permute-done.1), channel_id=1, source_target_pairs={{0,28},{4,0},{8,4},{12,8},{16,12},{20,16},{24,20},{28,24},{1,29},{... | collective-permute-start | bytes 3145736 | tf_op jit(solution)/shard_map/ppermute | solution.py:27
  97.4 28.6 %collective-permute-start.4 = (bf16[128,4096]{1,0:T(8,128)(2,1)}, bf16[128,4096]{1,0:T(8,128)(2,1)S(1)}, u32[]{:S(2)}, u32[]{:S(2)}) collective-permute-start(bf16[128,4096]{1,0:T(8,128)(2,1)} %collective-permute-done.2), channel_id=1, source_target_pairs={{0,4},{4,8},{8,12},{12,16},{16,20},{20,24},{24,28},{28,0},{1,5},{5... | collective-permute-start | bytes 3145736 | tf_op jit(solution)/shard_map/ppermute | solution.py:22
  102.5 27.2 %collective-permute-start.5 = (bf16[128,4096]{1,0:T(8,128)(2,1)S(1)}, bf16[128,4096]{1,0:T(8,128)(2,1)S(1)}, u32[]{:S(2)}, u32[]{:S(2)}) collective-permute-start(bf16[128,4096]{1,0:T(8,128)(2,1)S(1)} %collective-permute-done.3), channel_id=1, source_target_pairs={{0,28},{4,0},{8,4},{12,8},{16,12},{20,16},{24,20},{28,24},{1,29},{... | collective-permute-start | bytes 3145736 | tf_op jit(solution)/shard_map/ppermute | solution.py:27
  126.0 26.1 %collective-permute-start.6 = (bf16[128,4096]{1,0:T(8,128)(2,1)S(1)}, bf16[128,4096]{1,0:T(8,128)(2,1)S(1)}, u32[]{:S(2)}, u32[]{:S(2)}) collective-permute-start(bf16[128,4096]{1,0:T(8,128)(2,1)S(1)} %collective-permute-done.4), channel_id=1, source_target_pairs={{0,4},{4,8},{8,12},{12,16},{16,20},{20,24},{24,28},{28,0},{1,5},{5... | collective-permute-start | bytes 3145736 | tf_op jit(solution)/shard_map/ppermute | solution.py:22
  226.5 118.6 %collective-permute-start.22 = (bf16[4,512,1024]{2,1,0:T(8,128)(2,1)}, bf16[4,512,1024]{2,1,0:T(8,128)(2,1)}, u32[]{:S(2)}, u32[]{:S(2)}) collective-permute-start(bf16[4,512,1024]{2,1,0:T(8,128)(2,1)} %fusion.17), channel_id=1, source_target_pairs={{0,4},{4,0},{8,12},{12,8},{16,20},{20,16},{24,28},{28,24},{1,5},{5... | collective-permute-start | bytes 12582920 | tf_op jit(solution)/shard_map/ppermute | solution.py:101
  308.2 146.3 %collective-permute-start.17 = (bf16[4,128,4096]{2,1,0:T(8,128)(2,1)}, bf16[4,128,4096]{2,1,0:T(8,128)(2,1)}, u32[]{:S(2)}, u32[]{:S(2)}) collective-permute-start(bf16[4,128,4096]{2,1,0:T(8,128)(2,1)} %fusion.16), channel_id=1, source_target_pairs={{0,4},{4,0},{8,12},{12,8},{16,20},{20,16},{24,28},{28,24},{1,5},{5... | collective-permute-start | bytes 12582920 | tf_op jit(solution)/shard_map/ppermute | solution.py:101
  314.4 37.2 %collective-permute-start.12 = (bf16[4,128,1024]{2,1,0:T(8,128)(2,1)S(1)}, bf16[4,128,1024]{2,1,0:T(8,128)(2,1)}, u32[]{:S(2)}, u32[]{:S(2)}) collective-permute-start(bf16[4,128,1024]{2,1,0:T(8,128)(2,1)S(1)} %fusion.32), channel_id=1, source_target_pairs={{0,4},{4,0},{8,12},{12,8},{16,20},{20,16},{24,28},{28,24},{1,5},{5... | collective-permute-start | bytes 3145736 | tf_op jit(solution)/shard_map/ppermute | solution.py:101
  335.9 111.4 %collective-permute-start.7 = (bf16[4,128,3072]{2,1,0:T(8,128)(2,1)}, bf16[4,128,3072]{2,1,0:T(8,128)(2,1)}, u32[]{:S(2)}, u32[]{:S(2)}) collective-permute-start(bf16[4,128,3072]{2,1,0:T(8,128)(2,1)} %fusion.22), channel_id=1, source_target_pairs={{0,4},{4,0},{8,12},{12,8},{16,20},{20,16},{24,28},{28,24},{1,5},{5... | collective-permute-start | bytes 9437192 | tf_op jit(solution)/shard_map/ppermute | solution.py:101
  358.2 9.2 %collective-permute-start.15 = (bf16[2,64,1024]{2,1,0:T(8,128)(2,1)S(1)}, bf16[2,64,1024]{2,1,0:T(8,128)(2,1)S(1)}, u32[]{:S(2)}, u32[]{:S(2)}) collective-permute-start(bf16[2,64,1024]{2,1,0:T(8,128)(2,1)S(1)} %pad_maximum_fusion.13), channel_id=1, source_target_pairs={{0,16},{4,20},{8,24},{12,28},{16,0},{20,4},{24,8},{28,12},{1,17},{... | collective-permute-start | bytes 786440 | tf_op jit(solution)/shard_map/ppermute | solution.py:114
  359.1 8.9 %collective-permute-start.13 = (bf16[2,64,1024]{2,1,0:T(8,128)(2,1)S(1)}, bf16[2,64,1024]{2,1,0:T(8,128)(2,1)S(1)}, u32[]{:S(2)}, u32[]{:S(2)}) collective-permute-start(bf16[2,64,1024]{2,1,0:T(8,128)(2,1)S(1)} %pad_maximum_fusion.12), channel_id=1, source_target_pairs={{0,8},{4,12},{8,0},{12,4},{16,24},{20,28},{24,16},{28,20},{1,9},{5... | collective-permute-start | bytes 786440 | tf_op jit(solution)/shard_map/ppermute | solution.py:111
  361.5 75.4 %collective-permute-start.25 = (bf16[2,256,1024]{2,1,0:T(8,128)(2,1)}, bf16[2,256,1024]{2,1,0:T(8,128)(2,1)}, u32[]{:S(2)}, u32[]{:S(2)}) collective-permute-start(bf16[2,256,1024]{2,1,0:T(8,128)(2,1)} %pad_maximum_fusion.7), channel_id=1, source_target_pairs={{0,16},{4,20},{8,24},{12,28},{16,0},{20,4},{24,8},{28,12},{1,17},{... | collective-permute-start | bytes 3145736 | tf_op jit(solution)/shard_map/ppermute | solution.py:114
  367.4 70.8 %collective-permute-start.23 = (bf16[2,256,1024]{2,1,0:T(8,128)(2,1)}, bf16[2,256,1024]{2,1,0:T(8,128)(2,1)}, u32[]{:S(2)}, u32[]{:S(2)}) collective-permute-start(bf16[2,256,1024]{2,1,0:T(8,128)(2,1)} %pad_maximum_fusion.6), channel_id=1, source_target_pairs={{0,8},{4,12},{8,0},{12,4},{16,24},{20,28},{24,16},{28,20},{1,9},{5... | collective-permute-start | bytes 3145736 | tf_op jit(solution)/shard_map/ppermute | solution.py:111
  368.1 24.1 %collective-permute-start.14 = (bf16[64,1024]{1,0:T(8,128)(2,1)S(1)}, bf16[64,1024]{1,0:T(8,128)(2,1)S(1)}, u32[]{:S(2)}, u32[]{:S(2)}) collective-permute-start(bf16[64,1024]{1,0:T(8,128)(2,1)S(1)} %get-tuple-element.42), channel_id=1, source_target_pairs={{0,16},{4,20},{8,24},{12,28},{16,0},{20,4},{24,8},{28,12},{1,17},{... | collective-permute-start | bytes 393224 | tf_op jit(solution)/shard_map/ppermute | solution.py:121
  392.2 42.8 %collective-permute-start.16 = (bf16[64,1024]{1,0:T(8,128)(2,1)S(1)}, bf16[64,1024]{1,0:T(8,128)(2,1)S(1)}, u32[]{:S(2)}, u32[]{:S(2)}) collective-permute-start(bf16[64,1024]{1,0:T(8,128)(2,1)S(1)} %get-tuple-element.43), channel_id=1, source_target_pairs={{0,8},{4,12},{8,0},{12,4},{16,24},{20,28},{24,16},{28,20},{1,9},{5... | collective-permute-start | bytes 393224 | tf_op jit(solution)/shard_map/ppermute | solution.py:124
  443.3 18.4 %collective-permute-start.24 = (bf16[256,1024]{1,0:T(8,128)(2,1)}, bf16[256,1024]{1,0:T(8,128)(2,1)}, u32[]{:S(2)}, u32[]{:S(2)}) collective-permute-start(bf16[256,1024]{1,0:T(8,128)(2,1)} %get-tuple-element.21), channel_id=1, source_target_pairs={{0,16},{4,20},{8,24},{12,28},{16,0},{20,4},{24,8},{28,12},{1,17},{... | collective-permute-start | bytes 1572872 | tf_op jit(solution)/shard_map/ppermute | solution.py:121
  446.0 17.0 %collective-permute-start.26 = (bf16[256,1024]{1,0:T(8,128)(2,1)}, bf16[256,1024]{1,0:T(8,128)(2,1)}, u32[]{:S(2)}, u32[]{:S(2)}) collective-permute-start(bf16[256,1024]{1,0:T(8,128)(2,1)} %get-tuple-element.22), channel_id=1, source_target_pairs={{0,8},{4,12},{8,0},{12,4},{16,24},{20,28},{24,16},{28,20},{1,9},{5... | collective-permute-start | bytes 1572872 | tf_op jit(solution)/shard_map/ppermute | solution.py:124
  452.2 23.7 %collective-permute-start.10 = (bf16[2,64,3072]{2,1,0:T(8,128)(2,1)S(1)}, bf16[2,64,3072]{2,1,0:T(8,128)(2,1)}, u32[]{:S(2)}, u32[]{:S(2)}) collective-permute-start(bf16[2,64,3072]{2,1,0:T(8,128)(2,1)S(1)} %pad_maximum_fusion.10), channel_id=1, source_target_pairs={{0,16},{4,20},{8,24},{12,28},{16,0},{20,4},{24,8},{28,12},{1,17},{... | collective-permute-start | bytes 2359304 | tf_op jit(solution)/shard_map/ppermute | solution.py:114
  452.7 25.3 %collective-permute-start.8 = (bf16[2,64,3072]{2,1,0:T(8,128)(2,1)S(1)}, bf16[2,64,3072]{2,1,0:T(8,128)(2,1)}, u32[]{:S(2)}, u32[]{:S(2)}) collective-permute-start(bf16[2,64,3072]{2,1,0:T(8,128)(2,1)S(1)} %pad_maximum_fusion.9), channel_id=1, source_target_pairs={{0,8},{4,12},{8,0},{12,4},{16,24},{20,28},{24,16},{28,20},{1,9},{5... | collective-permute-start | bytes 2359304 | tf_op jit(solution)/shard_map/ppermute | solution.py:111
  460.8 37.5 %collective-permute-start.20 = (bf16[2,64,4096]{2,1,0:T(8,128)(2,1)S(1)}, bf16[2,64,4096]{2,1,0:T(8,128)(2,1)S(1)}, u32[]{:S(2)}, u32[]{:S(2)}) collective-permute-start(bf16[2,64,4096]{2,1,0:T(8,128)(2,1)S(1)} %pad_maximum_fusion.4), channel_id=1, source_target_pairs={{0,16},{4,20},{8,24},{12,28},{16,0},{20,4},{24,8},{28,12},{1,17},{... | collective-permute-start | bytes 3145736 | tf_op jit(solution)/shard_map/ppermute | solution.py:114
  461.7 38.7 %collective-permute-start.18 = (bf16[2,64,4096]{2,1,0:T(8,128)(2,1)S(1)}, bf16[2,64,4096]{2,1,0:T(8,128)(2,1)S(1)}, u32[]{:S(2)}, u32[]{:S(2)}) collective-permute-start(bf16[2,64,4096]{2,1,0:T(8,128)(2,1)S(1)} %pad_maximum_fusion.3), channel_id=1, source_target_pairs={{0,8},{4,12},{8,0},{12,4},{16,24},{20,28},{24,16},{28,20},{1,9},{5... | collective-permute-start | bytes 3145736 | tf_op jit(solution)/shard_map/ppermute | solution.py:111
  479.5 29.3 %collective-permute-start.11 = (bf16[64,3072]{1,0:T(8,128)(2,1)S(1)}, bf16[64,3072]{1,0:T(8,128)(2,1)S(1)}, u32[]{:S(2)}, u32[]{:S(2)}) collective-permute-start(bf16[64,3072]{1,0:T(8,128)(2,1)S(1)} %get-tuple-element.34), channel_id=1, source_target_pairs={{0,8},{4,12},{8,0},{12,4},{16,24},{20,28},{24,16},{28,20},{1,9},{5... | collective-permute-start | bytes 1179656 | tf_op jit(solution)/shard_map/ppermute | solution.py:124
  480.8 28.0 %collective-permute-start.9 = (bf16[64,3072]{1,0:T(8,128)(2,1)S(1)}, bf16[64,3072]{1,0:T(8,128)(2,1)S(1)}, u32[]{:S(2)}, u32[]{:S(2)}) collective-permute-start(bf16[64,3072]{1,0:T(8,128)(2,1)S(1)} %get-tuple-element.33), channel_id=1, source_target_pairs={{0,16},{4,20},{8,24},{12,28},{16,0},{20,4},{24,8},{28,12},{1,17},{... | collective-permute-start | bytes 1179656 | tf_op jit(solution)/shard_map/ppermute | solution.py:121
  500.8 15.3 %collective-permute-start.19 = (bf16[64,4096]{1,0:T(8,128)(2,1)S(1)}, bf16[64,4096]{1,0:T(8,128)(2,1)S(1)}, u32[]{:S(2)}, u32[]{:S(2)}) collective-permute-start(bf16[64,4096]{1,0:T(8,128)(2,1)S(1)} %get-tuple-element.27), channel_id=1, source_target_pairs={{0,16},{4,20},{8,24},{12,28},{16,0},{20,4},{24,8},{28,12},{1,17},{... | collective-permute-start | bytes 1572872 | tf_op jit(solution)/shard_map/ppermute | solution.py:121
  501.1 16.5 %collective-permute-start.21 = (bf16[64,4096]{1,0:T(8,128)(2,1)S(1)}, bf16[64,4096]{1,0:T(8,128)(2,1)S(1)}, u32[]{:S(2)}, u32[]{:S(2)}) collective-permute-start(bf16[64,4096]{1,0:T(8,128)(2,1)S(1)} %get-tuple-element.28), channel_id=1, source_target_pairs={{0,8},{4,12},{8,0},{12,4},{16,24},{20,28},{24,16},{28,20},{1,9},{5... | collective-permute-start | bytes 1572872 | tf_op jit(solution)/shard_map/ppermute | solution.py:124
  (56 other events, 1107.5 us)
Sparse Core Ops, SparseCore 0:
  9.9 70.1 all-gather.5
  81.9 33.4 all-gather.7
  117.3 60.3 all-gather.9
  519.2 120.0 all-reduce.2
